TPU v7x, 512 devices: a whole 4x4x16 slice. The times are simulated.
512 devices in a mesh: seq: 32 (over z, core), tensor: 16 (over y, x).
Axes of the slice: x: 4, y: 4, z: 16, core: 2. Of those that a mesh axis runs over, the one named last changes fastest.
Arguments:
- hidden: bfloat16 [4, 64, 5120], P(None, None, 'seq'), may hold values from -400 to 400
- norm_gain: bfloat16 [5120], P('seq'), may hold values from 0.099609375 to 1.8984375
- w_qkv: bfloat16 [5120, 7168], P('seq', 'tensor'), may hold values from -0.078125 to 0.078125
- b_qkv: bfloat16 [7168], P('tensor'), may hold values from -3 to 3
- w_out: bfloat16 [5120, 5120], P('tensor', 'seq'), may hold values from -0.078125 to 0.078125
- prefix_key_cache: bfloat16 [16, 12288, 1024], P('tensor', 'seq'), may hold values from -140 to 140
- prefix_value_cache: bfloat16 [16, 12288, 1024], P('tensor', 'seq'), may hold values from -6 to 6
- suffix_key_cache: bfloat16 [64, 4096, 1024], P('tensor', 'seq'), may hold values from -8 to 8
- suffix_value_cache: bfloat16 [64, 4096, 1024], P('tensor', 'seq'), may hold values from -6 to 6
- prefix_lens: int32 [16], P('tensor'), may hold values from 1 to 12288, as said below
- suffix_lens: int32 [64], P('tensor'), may hold values from 0 to 4096, as said below
Outputs:
- attn_out: float32 [4, 64, 5120], P(None, 'tensor', 'seq')
- new_keys: float32 [64, 4, 1024], P('tensor')
- new_values: float32 [64, 4, 1024], P('tensor')
Inputs may be any that keep to these rules, and one draw needn't show every extreme that they name: `prefix_lens`: some group has exactly 12288 live slots and some exactly one. `suffix_lens`: some request has exactly 4096 live slots and some none.
All inputs are finite; a program needn't handle non-finite values.
Results may differ from a plain program's by a relative error of at most 0.012.
The roundings to bfloat16 on the way count: a program that leaves them out, or rounds other values in their place, can miss the bound.
Values may be sent and summed in bfloat16 or wider, within the bound.
No kernel may reach another device: no remote copies, remote signals or barrier semaphores. Data moves between devices by JAX's collectives and lax.ppermute only.
A program may use at most 64 MiB of HBM per device.

v0:
```python
import jax
import jax.numpy as jnp
from jax import lax
from jax.sharding import PartitionSpec as P

D = 5120
QUERY_HEADS = 40
KEY_HEADS = 8
HEAD_SIZE = 128
KEY_COLUMNS = 1024
epsilon = 1e-06
masked_fill = -1e30


def apply_rotary(values, token_positions):
    half = values.shape[-1] // 2
    freq = jnp.exp(
        -(jnp.arange(half, dtype=jnp.float32) * (2.0 / values.shape[-1]))
        * jnp.log(jnp.float32(1000000.0))
    )
    angles = token_positions[..., None, None] * freq
    cosine = jnp.cos(angles)
    sine = jnp.sin(angles)
    left = values[..., :half]
    right = values[..., half:]
    return jnp.concatenate([left * cosine - right * sine, right * cosine + left * sine], axis=-1)


def body(
    hidden,
    norm_gain,
    w_qkv,
    b_qkv,
    w_out,
    prefix_key_cache,
    prefix_value_cache,
    suffix_key_cache,
    suffix_value_cache,
    prefix_lens,
    suffix_lens,
):
    decode_step_count = hidden.shape[0]
    request_count = suffix_lens.shape[0]
    prefix_count = prefix_key_cache.shape[1]
    suffix_count = suffix_key_cache.shape[1]
    query_group_width = QUERY_HEADS // KEY_HEADS
    query_width = QUERY_HEADS * HEAD_SIZE
    query_rows = decode_step_count * query_group_width
    scale = float(HEAD_SIZE) ** (-0.5)
    seq_index = lax.axis_index("seq")
    xf = hidden.astype(jnp.float32)
    squares = lax.psum(jnp.sum(xf * xf, axis=2), "seq")
    normed = (
        xf * lax.rsqrt(squares / D + epsilon)[..., None] * norm_gain.astype(jnp.float32)
    ).astype(jnp.bfloat16)
    partial_value = jnp.einsum("sbd,dc->sbc", normed, w_qkv, preferred_element_type=jnp.float32)
    bias = b_qkv.astype(jnp.float32)
    summed_cols = lax.psum(partial_value, "seq") + bias
    combined_output = lax.all_to_all(summed_cols, "tensor", split_axis=1, concat_axis=2, tiled=True)
    token_positions = (
        (prefix_lens[0] + suffix_lens)[None, :]
        + jnp.arange(decode_step_count, dtype=jnp.int32)[:, None]
    ).astype(jnp.float32)
    query_matrix = apply_rotary(
        combined_output[..., :query_width].reshape(
            decode_step_count, request_count, QUERY_HEADS, HEAD_SIZE
        ),
        token_positions,
    ).astype(jnp.bfloat16)
    keys_float = apply_rotary(
        combined_output[..., query_width : query_width + KEY_COLUMNS].reshape(
            decode_step_count, request_count, KEY_HEADS, HEAD_SIZE
        ),
        token_positions,
    )
    values_float = combined_output[..., query_width + KEY_COLUMNS :].reshape(
        decode_step_count, request_count, KEY_HEADS, HEAD_SIZE
    )
    current_keys = keys_float.astype(jnp.bfloat16)
    current_values = values_float.astype(jnp.bfloat16)
    new_keys = keys_float.reshape(decode_step_count, request_count, KEY_COLUMNS).transpose(1, 0, 2)
    new_values = values_float.reshape(decode_step_count, request_count, KEY_COLUMNS).transpose(
        1, 0, 2
    )
    query_by_group = (
        query_matrix.reshape(
            decode_step_count, request_count, KEY_HEADS, query_group_width, HEAD_SIZE
        )
        .transpose(1, 2, 0, 3, 4)
        .reshape(request_count, KEY_HEADS, query_rows, HEAD_SIZE)
    )
    prefix_key_block = prefix_key_cache[0].reshape(prefix_count, KEY_HEADS, HEAD_SIZE)
    prefix_value_block = prefix_value_cache[0].reshape(prefix_count, KEY_HEADS, HEAD_SIZE)
    suffix_key_block = suffix_key_cache.reshape(request_count, suffix_count, KEY_HEADS, HEAD_SIZE)
    suffix_value_block = suffix_value_cache.reshape(
        request_count, suffix_count, KEY_HEADS, HEAD_SIZE
    )
    score_pre = (
        jnp.einsum(
            "rhqd,phd->rhqp", query_by_group, prefix_key_block, preferred_element_type=jnp.float32
        )
        * scale
    )
    score_suf = (
        jnp.einsum(
            "rhqd,rshd->rhqs", query_by_group, suffix_key_block, preferred_element_type=jnp.float32
        )
        * scale
    )
    pre_mask = (
        seq_index * prefix_count + jnp.arange(prefix_count, dtype=jnp.int32) < prefix_lens[0]
    )[None, None, None, :]
    suf_mask = (
        (seq_index * suffix_count + jnp.arange(suffix_count, dtype=jnp.int32))[None, :]
        < suffix_lens[:, None]
    )[:, None, None, :]
    fill_pre = jnp.where(pre_mask, score_pre, masked_fill)
    fill_suf = jnp.where(suf_mask, score_suf, masked_fill)
    local_max = jnp.maximum(jnp.max(fill_pre, axis=3), jnp.max(fill_suf, axis=3))
    prob_pre = jnp.where(pre_mask, jnp.exp(fill_pre - local_max[..., None]), 0.0)
    prob_suf = jnp.where(suf_mask, jnp.exp(fill_suf - local_max[..., None]), 0.0)
    local_weight = jnp.sum(prob_pre, axis=3) + jnp.sum(prob_suf, axis=3)
    local_acc = jnp.einsum(
        "rhqp,phd->rhqd",
        prob_pre.astype(jnp.bfloat16),
        prefix_value_block,
        preferred_element_type=jnp.float32,
    )
    local_acc = local_acc + jnp.einsum(
        "rhqs,rshd->rhqd",
        prob_suf.astype(jnp.bfloat16),
        suffix_value_block,
        preferred_element_type=jnp.float32,
    )
    global_max = lax.pmax(local_max, "seq")
    factor = jnp.exp(local_max - global_max)
    global_weight, global_acc = lax.psum(
        (local_weight * factor, local_acc * factor[..., None]), "seq"
    )
    fresh_k = current_keys.transpose(1, 2, 0, 3)
    fresh_v = current_values.transpose(1, 2, 0, 3)
    score_new = (
        jnp.einsum("rhqd,rhid->rhqi", query_by_group, fresh_k, preferred_element_type=jnp.float32)
        * scale
    )
    new_mask = (
        (jnp.arange(query_rows, dtype=jnp.int32) // query_group_width)[:, None]
        >= jnp.arange(decode_step_count, dtype=jnp.int32)[None, :]
    )[None, None]
    fill_new = jnp.where(new_mask, score_new, masked_fill)
    new_max = jnp.max(fill_new, axis=3)
    prob_new = jnp.where(new_mask, jnp.exp(fill_new - new_max[..., None]), 0.0)
    top = jnp.maximum(global_max, new_max)
    factor_old = jnp.exp(global_max - top)
    factor_new = jnp.exp(new_max - top)
    total = global_weight * factor_old + jnp.sum(prob_new, axis=3) * factor_new
    new_acc = jnp.einsum(
        "rhqi,rhid->rhqd",
        prob_new.astype(jnp.bfloat16),
        fresh_v,
        preferred_element_type=jnp.float32,
    )
    summed = global_acc * factor_old[..., None] + new_acc * factor_new[..., None]
    attention_output = (summed / total[..., None]).astype(jnp.bfloat16)
    heads_local = (
        attention_output.reshape(
            request_count, KEY_HEADS, decode_step_count, query_group_width, HEAD_SIZE
        )
        .transpose(2, 0, 1, 3, 4)
        .reshape(decode_step_count, request_count, query_width)
    )
    by_heads = lax.all_to_all(heads_local, "tensor", split_axis=2, concat_axis=1, tiled=True)
    projected = jnp.einsum("sbc,cd->sbd", by_heads, w_out, preferred_element_type=jnp.float32)
    owned = lax.psum_scatter(projected, "tensor", scatter_dimension=1, tiled=True)
    return (owned, new_keys, new_values)


def solution(mesh):
    placed = (
        P(None, None, "seq"),
        P("seq"),
        P("seq", "tensor"),
        P("tensor"),
        P("tensor", "seq"),
        P("tensor", "seq", None),
        P("tensor", "seq", None),
        P("tensor", "seq", None),
        P("tensor", "seq", None),
        P("tensor"),
        P("tensor"),
    )
    return jax.shard_map(
        body,
        mesh=mesh,
        in_specs=placed,
        out_specs=(P(None, "tensor", "seq"), P("tensor", None, None), P("tensor", None, None)),
        check_vma=False,
    )
```

profile of v0, /device:TPU:2, one launch (start us, length us, event | category | flops | bytes accessed | tf_op | source)
XLA Modules:
  0.0 850.0 jit_solution(4505224170774639408)
XLA Ops:
  7.2 0.0 copy-start
  7.2 0.0 copy-start.19
  7.2 0.0 copy-start.16
  7.2 0.0 all-reduce.5.cloned.1.call-start
  7.3 0.8 convert_element_type.43
  8.0 1.0 fusion.22
  9.1 54.7 %psum.28 = f32[4,64]{1,0:T(4,128)S(1)} all-reduce(f32[4,64]{1,0:T(4,128)S(1)} %fusion.22), channel_id=1, replica_groups=mesh['seq'=32,'tensor'=16] {'seq'}, use_global_device_ids=true, to_apply=%region_1.0 | all-reduce | flops 256 | bytes 2048 | tf_op jit(solution)/shard_map/psum | solution.py:52
  63.8 2.1 fusion.29
  65.9 0.0 all-reduce.5.cloned.1.call-update
  66.6 0.1 add_convert_fusion.1
  66.6 0.1 multiply_cosine_fusion
  66.9 0.0 copy-done.4
  66.9 0.2 copy.148
  67.1 2.2 copy.149
  69.3 0.0 copy-done.13
  69.3 199.9 %all-reduce.5.cloned.1.call-done = f32[4,64,448]{2,1,0:T(8,128)} async-done(((f32[4,64,448]{2,1,0:T(8,128)}), f32[4,64,448]{2,1,0:T(8,128)}) %all-reduce.5.cloned.1.call-update) | async-done | bytes 458768 | tf_op jit(solution)/shard_map/psum | solution.py:58
  269.2 1.1 broadcast_add_fusion
  270.4 1.1 copy.98
  271.5 7.3 all-to-all-start
  278.8 0.0 all-reduce.7.cloned.1.call-start
  278.8 0.5 iota_compare_fusion
  279.4 0.1 broadcast_compare_fusion
  279.4 9.8 %all-to-all-done = f32[4,64,448]{2,0,1:T(4,128)S(1)} async-done(((f32[4,64,448]{2,0,1:T(4,128)}), f32[4,64,448]{2,0,1:T(4,128)S(1)}, u32[]{:S(2)}, u32[]{:S(2)}) %all-to-all-start) | async-done | bytes 458784 | tf_op jit(solution)/shard_map/all_to_all | solution.py:59
  289.2 0.3 copy.99
  289.5 0.3 all_to_all.29
  289.9 0.6 slice_bitcast_fusion.1
  290.6 0.1 reshape.150
  290.7 0.2 fusion.51
  290.9 0.4 subtract_convert_fusion
  291.3 0.2 maximum_bitcast_fusion
  291.6 1.4 fusion.52
  293.0 0.7 fusion.53
  293.7 0.0 copy-done.2
  293.7 91.2 %pmax.7 = f32[4,8,20]{2,1,0:T(8,128)} all-reduce(f32[4,8,20]{2,1,0:T(8,128)S(1)} %copy_maximum_fusion), channel_id=1, replica_groups=mesh['seq'=32,'tensor'=16] {'seq'}, use_global_device_ids=true, to_apply=%region_5.6 | all-reduce | flops 640 | bytes 5120 | tf_op jit(solution)/shard_map/pmax | solution.py:135
  384.9 1.5 multiply_subtract_fusion
  386.4 1.9 fusion.20
  388.2 1.1 fusion.12
  389.3 90.0 %psum.31 = f32[4,8,20]{2,1,0:T(8,128)S(1)} all-reduce(f32[4,8,20]{2,1,0:T(8,128)S(1)} %get-tuple-element.6), channel_id=1, replica_groups=mesh['seq'=32,'tensor'=16] {'seq'}, use_global_device_ids=true, to_apply=%region_10.11 | all-reduce | flops 640 | bytes 5120 | tf_op jit(solution)/shard_map/psum | solution.py:137
  479.4 1.3 convolution_bitcast_fusion
  480.7 0.0 copy-done.1
  480.7 0.0 copy-done.6
  480.7 0.0 copy-start.3
  480.7 0.0 copy-start.7
  480.8 1.2 fusion.4
  481.9 0.0 all-reduce.7.cloned.1.call-update
  481.9 0.0 all-reduce.9.cloned.1.call-start
  482.0 0.3 fusion.54
  482.3 0.1 fusion.37
  482.5 198.4 %all-reduce.7.cloned.1.call-done = f32[4,8,20,128]{3,2,0,1:T(8,128)} async-done(((f32[4,8,20,128]{3,2,0,1:T(8,128)}), f32[4,8,20,128]{3,2,0,1:T(8,128)}) %all-reduce.7.cloned.1.call-update) | async-done | bytes 327696 | tf_op jit(solution)/shard_map/psum | solution.py:137
  680.9 1.5 fusion.6
  682.3 0.1 copy.121
  682.4 4.5 copy.139
  686.9 11.0 %reshape.165 = bf16[16,2,2560]{2,1,0:T(2,128)(2,1)S(1)} reshape(bf16[5120,4,4]{2,1,0:T(4,128)(2,1)} %bitcast.84) | data formatting | bytes 327680
  697.9 13.9 %all_to_all.36 = bf16[16,2,2560]{2,1,0:T(2,128)(2,1)S(1)} all-to-all(bf16[16,2,2560]{2,1,0:T(2,128)(2,1)S(1)} %reshape.165), channel_id=1, replica_groups=mesh['seq'=32,'tensor'=16] {'tensor'}, dimensions={0} | all-to-all | bytes 327680 | tf_op jit(solution)/shard_map/all_to_all | solution.py:172
  711.8 12.3 %reshape.166 = bf16[5120,4,4]{2,1,0:T(4,128)(2,1)} reshape(bf16[16,2,2560]{2,1,0:T(2,128)(2,1)S(1)} %all_to_all.36) | data formatting | bytes 327680
  724.1 6.4 copy.140
  730.5 0.1 copy.125
  730.6 0.1 all_to_all.33
  730.7 0.9 fusion.34
  731.7 0.0 all-reduce.9.cloned.1.call-update
  731.7 1.3 dynamic-slice
  733.6 0.7 fusion.46
  734.4 107.7 %all-reduce.9.cloned.1.call-done = f32[4,64,160]{2,1,0:T(8,128)} async-done(((f32[4,64,160]{2,1,0:T(8,128)}), f32[4,64,160]{2,1,0:T(8,128)}) %all-reduce.9.cloned.1.call-update) | async-done | bytes 163856
  842.1 1.4 constant_dynamic-slice_fusion
  (49 shorter events, 0.2 us)
Async XLA Ops:
  7.2 284.4 %copy-start = (bf16[4,128,1024]{2,1,0:T(8,128)(2,1)S(1)}, bf16[4,128,1024]{2,1,0:T(8,128)(2,1)}, u32[]{:S(2)}) copy-start(bf16[4,128,1024]{2,1,0:T(8,128)(2,1)} %param.18) | copy-start | bytes 3145732
  7.2 59.4 %copy-start.19 = (s32[4]{0:T(128)S(1)}, s32[4]{0:T(128)}, u32[]{:S(2)}) copy-start(s32[4]{0:T(128)} %param.21) | copy-start | bytes 52
  7.2 59.6 %copy-start.16 = (bf16[448]{0:T(512)(128)(2,1)S(1)}, bf16[448]{0:T(512)(128)(2,1)}, u32[]{:S(2)}) copy-start(bf16[448]{0:T(512)(128)(2,1)} %param.14) | copy-start | bytes 2692
  7.2 59.7 %copy-start.4 = (bf16[1,384,1024]{2,1,0:T(8,128)(2,1)S(1)}, bf16[1,384,1024]{2,1,0:T(8,128)(2,1)}, u32[]{:S(2)}) copy-start(bf16[1,384,1024]{2,1,0:T(8,128)(2,1)} %param.16) | copy-start | bytes 2359300
  7.2 262.0 %all-reduce.5.cloned.1.call-start = ((), (), s32[]{:S(2)}) async-start(), calls=%async_computation.2 | async-start | bytes 1048576 | tf_op jit(solution)/shard_map/psum | solution.py:58
  66.8 2.5 copy-start.12
  66.8 2.5 copy-start.13
  69.3 223.7 %copy-start.15 = (pred[384]{0:T(512)(128)(4,1)}, pred[384]{0:T(512)(128)(4,1)S(1)}, u32[]{:S(2)}) copy-start(pred[384]{0:T(512)(128)(4,1)S(1)} %add_compare_fusion) | copy-start | bytes 1156
  271.5 17.7 %all-to-all-start = ((f32[4,64,448]{2,0,1:T(4,128)}), f32[4,64,448]{2,0,1:T(4,128)S(1)}, u32[]{:S(2)}, u32[]{:S(2)}) async-start(f32[4,64,448]{2,0,1:T(4,128)} %copy.98), calls=%async_computation | async-start | bytes 1048576 | tf_op jit(solution)/shard_map/all_to_all | solution.py:59
  278.8 402.1 %all-reduce.7.cloned.1.call-start = ((), (), s32[]{:S(2)}) async-start(), calls=%async_computation.3 | async-start | bytes 786432 | tf_op jit(solution)/shard_map/psum | solution.py:137
  279.4 12.2 %copy-start.18 = (pred[4,128]{1,0:T(4,128)(4,1)}, pred[4,128]{1,0:T(4,128)(4,1)S(1)}, u32[]{:S(2)}) copy-start(pred[4,128]{1,0:T(4,128)(4,1)S(1)} %broadcast_compare_fusion) | copy-start | bytes 1540
  291.6 2.1 copy-start.2
  293.7 185.6 %copy-start.5 = (bf16[48,8,8,128]{3,2,1,0:T(8,128)(2,1)S(1)}, bf16[48,8,8,128]{3,2,1,0:T(8,128)(2,1)}, u32[]{:S(2)}) copy-start(bf16[48,8,8,128]{3,2,1,0:T(8,128)(2,1)} %copy.149) | copy-start | bytes 2359300
  384.9 4.4 copy-start.9
  384.9 4.4 copy-start.14
  479.4 1.3 copy-start.1
  479.4 1.3 copy-start.6
  480.7 1.3 copy-start.3
  480.7 1.3 copy-start.7
  480.7 1.3 copy-start.8
  480.7 1.3 copy-start.17
  480.7 1.7 copy-start.10
  481.9 360.1 %all-reduce.9.cloned.1.call-start = ((), (), s32[]{:S(2)}) async-start(), calls=%async_computation.4 | async-start | bytes 524288
  724.1 6.6 copy-start.11
Sparse Core Ops, SparseCore 0:
  66.0 203.1 all-reduce.4
  482.1 198.7 all-reduce.6
  731.8 110.2 all-reduce.8
where the time goes:
time: 851 us; the launch traced here: 850 us
  waiting for transfers between devices  516 us (61%)
  blocking collectives  250 us (29%)
  local copies, waits for them, and re-layouts  42.4 us (5%)
  between operations  15.5 us (2%)
  other arithmetic  9.67 us (1%)
  matrix products  9.33 us (1%)
    psum x1, waiting for transfers between devices, body(): summed_cols = lax.psum(partial_value, 'seq') + bias  200 us
    psum x1, waiting for transfers between devices, body(): lax.psum((local_weight * factor, local_acc * factor[..., None]), 'seq')  198 us
    unnamed x4, waiting for transfers between devices  108 us
    pmax x1, blocking collectives, body(): global_max = lax.pmax(local_max, 'seq')  91.2 us
    psum x1, blocking collectives, body(): lax.psum((local_weight * factor, local_acc * factor[..., None]), 'seq')  90 us
    psum x1, blocking collectives, body(): squares = lax.psum(jnp.sum(xf * xf, axis=2), 'seq')  54.7 us
    unnamed x46, local copies, waits for them, and re-layouts  28.4 us
  transfers between devices with their start and end apart: 4, of which 4 were waited for; matrix products, arithmetic and copies ran while one was open for 1% of the time, Pallas kernels for 0%

commit v1 on v0

--- a/solution.py
+++ b/solution.py
@@ -169,7 +169,12 @@
         .transpose(2, 0, 1, 3, 4)
         .reshape(decode_step_count, request_count, query_width)
     )
-    by_heads = lax.all_to_all(heads_local, "tensor", split_axis=2, concat_axis=1, tiled=True)
+    by_heads = jnp.concatenate(
+        lax.all_to_all(
+            jnp.stack(jnp.split(heads_local, lax.axis_size("tensor"), axis=2)), "tensor", 0, 0
+        ),
+        axis=1,
+    )
     projected = jnp.einsum("sbc,cd->sbd", by_heads, w_out, preferred_element_type=jnp.float32)
     owned = lax.psum_scatter(projected, "tensor", scatter_dimension=1, tiled=True)
     return (owned, new_keys, new_values)

time: 851 us -> 818 us (0.961)
  local copies, waits for them, and re-layouts: 42.4 us -> 9.09 us
    unnamed x46 -> x59, local copies, waits for them, and re-layouts: 28.4 us -> 5.82 us
where the time goes in v1:
time: 818 us; the launch traced here: 817 us
  waiting for transfers between devices  516 us (63%)
  blocking collectives  250 us (31%)
  between operations  15.6 us (2%)
  other arithmetic  9.67 us (1%)
  matrix products  9.33 us (1%)
  local copies, waits for them, and re-layouts  9.09 us (1%)
    psum x1, waiting for transfers between devices, body(): summed_cols = lax.psum(partial_value, 'seq') + bias  200 us
    psum x1, waiting for transfers between devices, body(): lax.psum((local_weight * factor, local_acc * factor[..., None]), 'seq')  198 us
    unnamed x4, waiting for transfers between devices  108 us
    pmax x1, blocking collectives, body(): global_max = lax.pmax(local_max, 'seq')  91.2 us
    psum x1, blocking collectives, body(): lax.psum((local_weight * factor, local_acc * factor[..., None]), 'seq')  90 us
    psum x1, blocking collectives, body(): squares = lax.psum(jnp.sum(xf * xf, axis=2), 'seq')  54.7 us
  transfers between devices with their start and end apart: 4, of which 4 were waited for; matrix products, arithmetic and copies ran while one was open for 1% of the time, Pallas kernels for 0%

profile of v1, /device:TPU:2, one launch (start us, length us, event | category | flops | bytes accessed | tf_op | source)
XLA Modules:
  0.0 816.9 jit_solution(3058243633366432471)
XLA Ops:
  7.2 0.0 copy-start
  7.2 0.0 all-reduce.5.cloned.1.call-start
  7.3 0.8 convert_element_type.43
  8.0 1.0 fusion.22
  9.1 54.7 %psum.28 = f32[4,64]{1,0:T(4,128)S(1)} all-reduce(f32[4,64]{1,0:T(4,128)S(1)} %fusion.22), channel_id=1, replica_groups=mesh['seq'=32,'tensor'=16] {'seq'}, use_global_device_ids=true, to_apply=%region_1.0 | all-reduce | flops 256 | bytes 2048 | tf_op jit(solution)/shard_map/psum | solution.py:52
  63.8 2.1 fusion.29
  65.9 0.0 all-reduce.5.cloned.1.call-update
  66.6 0.0 copy-done.19
  66.6 0.1 add_convert_fusion.1
  66.6 0.1 multiply_cosine_fusion
  66.9 0.2 copy.154
  67.1 2.2 copy.155
  69.3 199.9 %all-reduce.5.cloned.1.call-done = f32[4,64,448]{2,1,0:T(8,128)} async-done(((f32[4,64,448]{2,1,0:T(8,128)}), f32[4,64,448]{2,1,0:T(8,128)}) %all-reduce.5.cloned.1.call-update) | async-done | bytes 458768 | tf_op jit(solution)/shard_map/psum | solution.py:58
  269.2 1.1 broadcast_add_fusion
  270.4 1.1 copy.109
  271.5 7.3 all-to-all-start
  278.8 0.0 all-reduce.7.cloned.1.call-start
  278.8 0.5 iota_compare_fusion
  279.4 0.1 broadcast_compare_fusion
  279.4 9.8 %all-to-all-done = f32[4,64,448]{2,0,1:T(4,128)S(1)} async-done(((f32[4,64,448]{2,0,1:T(4,128)}), f32[4,64,448]{2,0,1:T(4,128)S(1)}, u32[]{:S(2)}, u32[]{:S(2)}) %all-to-all-start) | async-done | bytes 458784 | tf_op jit(solution)/shard_map/all_to_all | solution.py:59
  289.2 0.3 copy.110
  289.6 0.3 all_to_all.19
  289.9 0.6 slice_bitcast_fusion.1
  290.6 0.1 reshape.156
  290.7 0.2 fusion.51
  290.9 0.4 subtract_convert_fusion
  291.3 0.2 maximum_bitcast_fusion
  291.6 1.4 fusion.52
  293.0 0.7 fusion.53
  293.7 91.2 %pmax.7 = f32[4,8,20]{2,1,0:T(8,128)} all-reduce(f32[4,8,20]{2,1,0:T(8,128)S(1)} %copy_maximum_fusion), channel_id=1, replica_groups=mesh['seq'=32,'tensor'=16] {'seq'}, use_global_device_ids=true, to_apply=%region_5.6 | all-reduce | flops 640 | bytes 5120 | tf_op jit(solution)/shard_map/pmax | solution.py:135
  384.9 1.5 multiply_subtract_fusion
  386.4 1.9 fusion.20
  388.2 1.1 fusion.12
  389.3 90.0 %psum.31 = f32[4,8,20]{2,1,0:T(8,128)S(1)} all-reduce(f32[4,8,20]{2,1,0:T(8,128)S(1)} %get-tuple-element.6), channel_id=1, replica_groups=mesh['seq'=32,'tensor'=16] {'seq'}, use_global_device_ids=true, to_apply=%region_10.11 | all-reduce | flops 640 | bytes 5120 | tf_op jit(solution)/shard_map/psum | solution.py:137
  479.4 1.3 convolution_bitcast_fusion
  480.7 0.0 copy-start.7
  480.8 1.2 fusion.4
  481.9 0.0 all-reduce.7.cloned.1.call-update
  481.9 0.0 all-reduce.9.cloned.1.call-start
  482.0 0.3 fusion.54
  482.3 0.1 fusion.37
  482.5 198.4 %all-reduce.7.cloned.1.call-done = f32[4,8,20,128]{3,2,0,1:T(8,128)} async-done(((f32[4,8,20,128]{3,2,0,1:T(8,128)}), f32[4,8,20,128]{3,2,0,1:T(8,128)}) %all-reduce.7.cloned.1.call-update) | async-done | bytes 327696 | tf_op jit(solution)/shard_map/psum | solution.py:137
  680.9 1.5 fusion.6
  682.4 0.1 copy.132
  682.4 0.0 copy-start.11
  682.4 0.1 copy.133
  682.5 0.1 reshape.162
  682.6 0.1 constant_dynamic-update-slice_fusion.14
  682.7 0.1 constant_dynamic-update-slice_fusion.12
  682.8 0.1 constant_dynamic-update-slice_fusion.10
  683.0 0.1 constant_dynamic-update-slice_fusion.8
  683.1 0.1 constant_dynamic-update-slice_fusion.6
  683.2 0.1 constant_dynamic-update-slice_fusion.4
  683.3 0.1 constant_dynamic-update-slice_fusion.2
  683.4 0.1 constant_dynamic-update-slice_fusion
  683.5 14.0 %all_to_all.23 = bf16[16,4,4,320]{3,2,1,0:T(4,128)(2,1)S(1)} all-to-all(bf16[16,4,4,320]{3,2,1,0:T(4,128)(2,1)S(1)} %constant_dynamic-update-slice_fusion), channel_id=1, replica_groups=mesh['seq'=32,'tensor'=16] {'tensor'}, dimensions={0} | all-to-all | bytes 327680 | tf_op jit(solution)/shard_map/all_to_all | solution.py:173
  697.5 0.1 copy.134
  697.6 0.1 reshape.164
  697.7 0.9 fusion.34
  698.6 0.0 all-reduce.9.cloned.1.call-update
  698.7 1.3 dynamic-slice
  700.6 0.7 fusion.46
  701.3 107.7 %all-reduce.9.cloned.1.call-done = f32[4,64,160]{2,1,0:T(8,128)} async-done(((f32[4,64,160]{2,1,0:T(8,128)}), f32[4,64,160]{2,1,0:T(8,128)}) %all-reduce.9.cloned.1.call-update) | async-done | bytes 163856
  809.0 1.4 constant_dynamic-slice_fusion
  (63 shorter events, 0.3 us)
Async XLA Ops:
  7.2 284.4 %copy-start = (bf16[4,128,1024]{2,1,0:T(8,128)(2,1)S(1)}, bf16[4,128,1024]{2,1,0:T(8,128)(2,1)}, u32[]{:S(2)}) copy-start(bf16[4,128,1024]{2,1,0:T(8,128)(2,1)} %param.18) | copy-start | bytes 3145732
  7.2 59.4 %copy-start.19 = (s32[4]{0:T(128)S(1)}, s32[4]{0:T(128)}, u32[]{:S(2)}) copy-start(s32[4]{0:T(128)} %param.21) | copy-start | bytes 52
  7.2 59.6 %copy-start.16 = (bf16[448]{0:T(512)(128)(2,1)S(1)}, bf16[448]{0:T(512)(128)(2,1)}, u32[]{:S(2)}) copy-start(bf16[448]{0:T(512)(128)(2,1)} %param.14) | copy-start | bytes 2692
  7.2 59.7 %copy-start.4 = (bf16[1,384,1024]{2,1,0:T(8,128)(2,1)S(1)}, bf16[1,384,1024]{2,1,0:T(8,128)(2,1)}, u32[]{:S(2)}) copy-start(bf16[1,384,1024]{2,1,0:T(8,128)(2,1)} %param.16) | copy-start | bytes 2359300
  7.2 262.0 %all-reduce.5.cloned.1.call-start = ((), (), s32[]{:S(2)}) async-start(), calls=%async_computation.2 | async-start | bytes 1048576 | tf_op jit(solution)/shard_map/psum | solution.py:58
  66.8 2.5 copy-start.13
  66.8 222.4 %copy-start.12 = (f32[4,4,64]{2,0,1:T(4,128)}, f32[4,4,64]{2,0,1:T(4,128)S(1)}, u32[]{:S(2)}) copy-start(f32[4,4,64]{2,0,1:T(4,128)S(1)} %get-tuple-element.20) | copy-start | bytes 12292
  69.3 223.7 %copy-start.15 = (pred[384]{0:T(512)(128)(4,1)}, pred[384]{0:T(512)(128)(4,1)S(1)}, u32[]{:S(2)}) copy-start(pred[384]{0:T(512)(128)(4,1)S(1)} %add_compare_fusion) | copy-start | bytes 1156
  271.5 17.7 %all-to-all-start = ((f32[4,64,448]{2,0,1:T(4,128)}), f32[4,64,448]{2,0,1:T(4,128)S(1)}, u32[]{:S(2)}, u32[]{:S(2)}) async-start(f32[4,64,448]{2,0,1:T(4,128)} %copy.109), calls=%async_computation | async-start | bytes 1048576 | tf_op jit(solution)/shard_map/all_to_all | solution.py:59
  278.8 402.1 %all-reduce.7.cloned.1.call-start = ((), (), s32[]{:S(2)}) async-start(), calls=%async_computation.3 | async-start | bytes 786432 | tf_op jit(solution)/shard_map/psum | solution.py:137
  279.4 12.2 %copy-start.18 = (pred[4,128]{1,0:T(4,128)(4,1)}, pred[4,128]{1,0:T(4,128)(4,1)S(1)}, u32[]{:S(2)}) copy-start(pred[4,128]{1,0:T(4,128)(4,1)S(1)} %broadcast_compare_fusion) | copy-start | bytes 1540
  291.6 2.1 copy-start.2
  293.7 185.6 %copy-start.5 = (bf16[48,8,8,128]{3,2,1,0:T(8,128)(2,1)S(1)}, bf16[48,8,8,128]{3,2,1,0:T(8,128)(2,1)}, u32[]{:S(2)}) copy-start(bf16[48,8,8,128]{3,2,1,0:T(8,128)(2,1)} %copy.155) | copy-start | bytes 2359300
  384.9 4.4 copy-start.9
  384.9 4.4 copy-start.14
  479.4 1.3 copy-start.1
  479.4 1.3 copy-start.6
  480.7 1.3 copy-start.3
  480.7 1.3 copy-start.7
  480.7 1.3 copy-start.8
  480.7 1.3 copy-start.17
  480.8 1.7 copy-start.10
  481.9 327.1 %all-reduce.9.cloned.1.call-start = ((), (), s32[]{:S(2)}) async-start(), calls=%async_computation.4 | async-start | bytes 524288
  682.4 15.2 %copy-start.11 = (bf16[320,160]{0,1:T(8,128)(2,1)S(1)}, bf16[320,160]{0,1:T(8,128)(2,1)}, u32[]{:S(2)}) copy-start(bf16[320,160]{0,1:T(8,128)(2,1)} %param.15) | copy-start | bytes 307204
Sparse Core Ops, SparseCore 0:
  66.0 203.1 all-reduce.4
  482.1 198.7 all-reduce.6
  698.8 110.1 all-reduce.8
